TPU v7x, 256 devices: a whole 4x4x8 slice. The times are simulated.
256 devices in a mesh: feeder: 32 (over z_hi, y, core), factor: 8 (over z_lo, x).
Axes of the slice: x: 4, y: 4, z: 8 (z_hi: 4, z_lo: 2; z = z_hi * 2 + z_lo), core: 2. Of those that a mesh axis runs over, the one named last changes fastest.
Arguments:
- sensitivity: bfloat16 [32, 2048, 2048], P('feeder'), may hold values from -0.015625 to 0.015625
- headroom: float32 [32, 8, 2048], P('feeder'), may hold values from 0 to 3
- ev_power: float32 [32, 8, 256], P('feeder'), may hold values from 0.5 to 4
- ev_node: int32 [32, 8, 256], P('feeder'), may hold values from 0 to 2047
- region_map: int32 [32, 256], P('feeder'), may hold values from 0 to 511
- loadings: float32 [512, 8, 512], P('feeder', None, 'factor'), may hold values from -8 to 8
Outputs:
- margin: float32 [32, 8, 2048], P('feeder')
- new_loadings: float32 [512, 8, 512], P('feeder', None, 'factor')
All inputs are finite; a program needn't handle non-finite values.
Results may differ from a plain program's by a relative error of at most 0.0031.
Values may be sent and summed in bfloat16 or wider, within the bound.
No kernel may reach another device: no remote copies, remote signals or barrier semaphores. Data moves between devices by JAX's collectives and lax.ppermute only.
A program may use at most 64 MiB of HBM per device.

v0:
```python
import jax
import jax.numpy as jnp
from jax import lax
from jax.sharding import PartitionSpec as P

quantile = 1.645
epsilon = 1e-06
step_size = 16.0


def shards(sensitivity, headroom, ev_power, ev_node, region_map, loadings):
    members = sensitivity.shape[0]
    ev_count = ev_power.shape[2]
    reg_local, hours, columns = loadings.shape
    total_regions = reg_local * lax.axis_size("feeder")
    packed = loadings.astype(jnp.bfloat16).reshape(reg_local, hours * columns)
    regions = region_map.reshape(-1)
    shard_rows = lax.all_gather(packed, "feeder", axis=0, tiled=True)
    row_count = shard_rows.shape[0]
    matches = (regions[:, None] == lax.iota(jnp.int32, row_count)[None, :]).astype(jnp.bfloat16)
    looked = jnp.dot(matches, shard_rows, preferred_element_type=jnp.float32)
    volts_list = []
    rows_list = []
    partial_list = []
    member = 0
    for interval in range(hours):
        block = looked[
            member * ev_count : (member + 1) * ev_count,
            interval * columns : (interval + 1) * columns,
        ]
        weighted = (ev_power[member, interval][:, None] * block).astype(jnp.bfloat16)
        sens_rows = jnp.take(sensitivity[member], ev_node[member, interval], axis=0)
        factor_volts = jnp.dot(weighted.T, sens_rows, preferred_element_type=jnp.float32)
        volts_list.append(factor_volts)
        rows_list.append(sens_rows)
        partial_sum = jnp.sum(factor_volts * factor_volts, axis=0)
        partial_list.append(partial_sum)
    variance = jnp.stack(partial_list, axis=0).reshape(members, hours, -1)
    variance = lax.psum(variance, "factor")
    deviation = jnp.sqrt(variance + epsilon)
    margin = headroom - quantile * deviation
    violation = jnp.maximum(-margin, 0.0)
    var_grad = quantile * violation / deviation
    member = 0
    interval_grads = []
    for interval in range(hours):
        position = member * hours + interval
        volt_grad = (2.0 * var_grad[member, interval][None, :] * volts_list[position]).astype(
            jnp.bfloat16
        )
        weight_grad = jnp.dot(rows_list[position], volt_grad.T, preferred_element_type=jnp.float32)
        interval_grads.append(ev_power[member, interval][:, None] * weight_grad)
    member_grads = jnp.concatenate(interval_grads, axis=1)
    offset = regions - 0
    inside = jnp.logical_and(offset >= 0, offset < total_regions)
    target = jnp.where(inside, offset, total_regions)
    summed = jax.ops.segment_sum(member_grads, target, num_segments=total_regions + 1)
    whole_term = summed[:total_regions]
    reduced = lax.psum_scatter(whole_term, "feeder", scatter_dimension=0, tiled=True)
    new_loadings = loadings - step_size * reduced.reshape(reg_local, hours, columns)
    return (margin, new_loadings)


def solution(mesh):
    return jax.shard_map(
        shards,
        mesh=mesh,
        in_specs=(
            P("feeder", None, None),
            P("feeder", None, None),
            P("feeder", None, None),
            P("feeder", None, None),
            P("feeder", None),
            P("feeder", None, "factor"),
        ),
        out_specs=(P("feeder", None, None), P("feeder", None, "factor")),
        check_vma=False,
    )
```

profile of v0, /device:TPU:2, one launch (start us, length us, event | category | flops | bytes accessed | tf_op | source)
XLA Modules:
  0.0 324.0 jit_solution(15895754559689770932)
XLA Ops:
  10.4 49.2 %all_gather.3 = bf16[512,512]{1,0:T(8,128)(2,1)S(1)} all-gather(bf16[16,512]{1,0:T(8,128)(2,1)S(1)} %reshape.133), channel_id=1, replica_groups=mesh['feeder'=32,'factor'=8] {'feeder'}, dimensions={0}, use_global_device_ids=true | all-gather | bytes 540672 | tf_op jit(solution)/shard_map/all_gather | solution.py:18
  59.6 6.8 %gather_fusion.2 = bf16[256,2048]{1,0:T(8,128)(2,1)S(1)} fusion(bf16[2048,2048]{1,0:T(8,128)(2,1)} %bitcast.39, s32[1024]{0:T(1024)S(1)} %pad_clamp_fusion.5), kind=kCustom, calls=%fused_computation.2.clone | custom fusion | bytes 2098176 | tf_op jit(solution)/shard_map/jit(_take)/gather | solution.py:32
  66.4 6.8 %gather_fusion.3 = bf16[256,2048]{1,0:T(8,128)(2,1)S(1)} fusion(bf16[2048,2048]{1,0:T(8,128)(2,1)} %bitcast.40, s32[1024]{0:T(1024)S(1)} %pad_clamp_fusion.4), kind=kCustom, calls=%fused_computation.3.clone | custom fusion | bytes 2098176 | tf_op jit(solution)/shard_map/jit(_take)/gather | solution.py:32
  73.3 7.8 %gather_fusion.4 = bf16[256,2048]{1,0:T(8,128)(2,1)} fusion(bf16[2048,2048]{1,0:T(8,128)(2,1)} %bitcast.41, s32[1024]{0:T(1024)S(1)} %pad_clamp_fusion.3), kind=kCustom, calls=%fused_computation.4.clone | custom fusion | bytes 2098176 | tf_op jit(solution)/shard_map/jit(_take)/gather | solution.py:32
  81.1 8.0 %gather_fusion.5 = bf16[256,2048]{1,0:T(8,128)(2,1)} fusion(bf16[2048,2048]{1,0:T(8,128)(2,1)} %bitcast.42, s32[1024]{0:T(1024)S(1)} %pad_clamp_fusion.2), kind=kCustom, calls=%fused_computation.5.clone | custom fusion | bytes 2098176 | tf_op jit(solution)/shard_map/jit(_take)/gather | solution.py:32
  89.1 7.8 %gather_fusion.6 = bf16[256,2048]{1,0:T(8,128)(2,1)} fusion(bf16[2048,2048]{1,0:T(8,128)(2,1)} %bitcast.43, s32[1024]{0:T(1024)S(1)} %pad_clamp_fusion.1), kind=kCustom, calls=%fused_computation.6.clone | custom fusion | bytes 2098176 | tf_op jit(solution)/shard_map/jit(_take)/gather | solution.py:32
  96.9 7.8 %gather_fusion.7 = bf16[256,2048]{1,0:T(8,128)(2,1)} fusion(bf16[2048,2048]{1,0:T(8,128)(2,1)} %bitcast.44, s32[1024]{0:T(1024)S(1)} %pad_clamp_fusion), kind=kCustom, calls=%fused_computation.7.clone | custom fusion | bytes 2098176 | tf_op jit(solution)/shard_map/jit(_take)/gather | solution.py:32
  104.7 7.9 %gather_fusion.1 = bf16[256,2048]{1,0:T(8,128)(2,1)} fusion(bf16[2048,2048]{1,0:T(8,128)(2,1)} %bitcast.45, s32[1024]{0:T(1024)S(1)} %pad_clamp_fusion.6), kind=kCustom, calls=%fused_computation.1.clone | custom fusion | bytes 2098176 | tf_op jit(solution)/shard_map/jit(_take)/gather | solution.py:32
  112.6 8.0 %gather_fusion = bf16[256,2048]{1,0:T(8,128)(2,1)} fusion(bf16[2048,2048]{1,0:T(8,128)(2,1)} %bitcast.46, s32[1024]{0:T(1024)S(1)} %pad_clamp_fusion.7), kind=kCustom, calls=%fused_computation.clone | custom fusion | bytes 2098176 | tf_op jit(solution)/shard_map/jit(_take)/gather | solution.py:32
  123.5 2.5 multiply_reduce_fusion.3
  126.0 2.6 multiply_reduce_fusion.2
  128.5 2.4 multiply_reduce_fusion.1
  131.0 1.3 multiply_reduce_fusion
  132.2 1.3 multiply_reduce_fusion.6
  133.5 1.2 multiply_reduce_fusion.7
  135.6 71.0 %all-reduce.2.cloned.1.call-done = f32[1,8,2048]{2,1,0:T(8,128)} async-done(((f32[1,8,2048]{2,1,0:T(8,128)}), f32[1,8,2048]{2,1,0:T(8,128)}) %all-reduce.2.cloned.1.call-update) | async-done | bytes 65552 | tf_op jit(solution)/shard_map/psum | solution.py:39
  206.6 1.6 multiply_divide_fusion
  208.3 2.0 convolution_multiply_fusion
  210.2 1.8 convolution_multiply_fusion.1
  212.1 2.5 convolution_multiply_fusion.2
  214.5 2.5 convolution_multiply_fusion.3
  219.8 1.3 concatenate.3
  221.1 2.3 scatter_custom_fusion
  224.5 91.1 %reduce-scatter.2.cloned.1.call-done = f32[16,512]{1,0:T(8,128)} async-done(((f32[512,512]{1,0:T(8,128)}), f32[16,512]{1,0:T(8,128)}) %reduce-scatter.2.cloned.1.call-update) | async-done | bytes 32784 | tf_op jit(solution)/shard_map/reduce_scatter | solution.py:59
  (70 shorter events, 12.0 us)
Async XLA Ops:
  7.2 199.4 %all-reduce.2.cloned.1.call-start = ((), (), s32[]{:S(2)}) async-start(), calls=%async_computation.1 | async-start | bytes 131072 | tf_op jit(solution)/shard_map/psum | solution.py:39
  104.7 15.9 %copy-start.7 = (s32[1,256]{1,0:T(1,128)S(1)}, s32[1,256]{1,0:T(1,128)}, u32[]{:S(2)}) copy-start(s32[1,256]{1,0:T(1,128)} %param.12) | copy-start | bytes 3076
  120.6 10.4 %copy-start.4 = (bf16[256,2048]{1,0:T(8,128)(2,1)S(1)}, bf16[256,2048]{1,0:T(8,128)(2,1)}, u32[]{:S(2)}) copy-start(bf16[256,2048]{1,0:T(8,128)(2,1)} %gather_fusion.7) | copy-start | bytes 3145732
  120.6 11.6 %copy-start.2 = (bf16[256,2048]{1,0:T(8,128)(2,1)S(1)}, bf16[256,2048]{1,0:T(8,128)(2,1)}, u32[]{:S(2)}) copy-start(bf16[256,2048]{1,0:T(8,128)(2,1)} %gather_fusion.1) | copy-start | bytes 3145732
  120.6 12.9 %copy-start = (bf16[256,2048]{1,0:T(8,128)(2,1)S(1)}, bf16[256,2048]{1,0:T(8,128)(2,1)}, u32[]{:S(2)}) copy-start(bf16[256,2048]{1,0:T(8,128)(2,1)} %gather_fusion) | copy-start | bytes 3145732
  120.6 85.9 %copy-start.6 = (f32[1,8,2048]{2,1,0:T(8,128)S(1)}, f32[1,8,2048]{2,1,0:T(8,128)}, u32[]{:S(2)}) copy-start(f32[1,8,2048]{2,1,0:T(8,128)} %param.9) | copy-start | bytes 196612
  133.5 85.2 %copy-start.3 = (bf16[256,2048]{1,0:T(8,128)(2,1)S(1)}, bf16[256,2048]{1,0:T(8,128)(2,1)}, u32[]{:S(2)}) copy-start(bf16[256,2048]{1,0:T(8,128)(2,1)} %gather_fusion.1) | copy-start | bytes 3145732
  135.5 180.1 %reduce-scatter.2.cloned.1.call-start = ((), (), s32[]{:S(2)}) async-start(), calls=%async_computation.2 | async-start | bytes 1081344 | tf_op jit(solution)/shard_map/reduce_scatter | solution.py:59
  206.5 10.5 %copy-start.10 = (f32[64,2048]{1,0:T(8,128)S(1)}, f32[64,2048]{1,0:T(8,128)}, u32[]{:S(2)}) copy-start(f32[64,2048]{1,0:T(8,128)} %get-tuple-element.36) | copy-start | bytes 1572868
  206.5 11.7 %copy-start.8 = (f32[64,2048]{1,0:T(8,128)S(1)}, f32[64,2048]{1,0:T(8,128)}, u32[]{:S(2)}) copy-start(f32[64,2048]{1,0:T(8,128)} %get-tuple-element.34) | copy-start | bytes 1572868
  206.5 12.2 %copy-start.11 = (f32[64,2048]{1,0:T(8,128)S(1)}, f32[64,2048]{1,0:T(8,128)}, u32[]{:S(2)}) copy-start(f32[64,2048]{1,0:T(8,128)} %get-tuple-element.32) | copy-start | bytes 1572868
  208.2 11.0 %copy-start.1 = (bf16[256,2048]{1,0:T(8,128)(2,1)S(1)}, bf16[256,2048]{1,0:T(8,128)(2,1)}, u32[]{:S(2)}) copy-start(bf16[256,2048]{1,0:T(8,128)(2,1)} %gather_fusion) | copy-start | bytes 3145732
  208.2 11.0 %copy-start.9 = (f32[64,2048]{1,0:T(8,128)S(1)}, f32[64,2048]{1,0:T(8,128)}, u32[]{:S(2)}) copy-start(f32[64,2048]{1,0:T(8,128)} %get-tuple-element.30) | copy-start | bytes 1572868
  214.5 101.9 %copy-start.5 = (f32[16,8,64]{2,1,0:T(8,128)S(1)}, f32[16,8,64]{2,1,0:T(8,128)}, u32[]{:S(2)}) copy-start(f32[16,8,64]{2,1,0:T(8,128)} %param.13) | copy-start | bytes 98308
Sparse Core Ops, SparseCore 0:
  135.6 70.8 all-reduce.1
  224.6 90.9 reduce-scatter.1
where the time goes:
time: 325 us; the launch traced here: 324 us
  waiting for transfers between devices  162 us (50%)
  local copies, waits for them, and re-layouts  66.3 us (20%)
  blocking collectives  49.2 us (15%)
  matrix products  25.5 us (8%)
  between operations  14.3 us (4%)
  other arithmetic  6.4 us (2%)
    reduce_scatter x1, waiting for transfers between devices, shards(): lax.psum_scatter(whole_term, 'feeder', scatter_dimension=0, tiled=True)  91.1 us
    psum x1, waiting for transfers between devices, shards(): variance = lax.psum(variance, 'factor')  71 us
    gather x8, local copies, waits for them, and re-layouts, shards(): sens_rows = jnp.take(sensitivity[member], ev_node[member, interval], axis=0)  61 us
    all_gather x1, blocking collectives, shards(): shard_rows = lax.all_gather(packed, 'feeder', axis=0, tiled=True)  49.2 us
    dot_general x8, matrix products, shards(): jnp.dot(weighted.T, sens_rows, preferred_element_type=jnp.float32)  13.7 us
    dot_general x8, matrix products, shards(): jnp.dot(rows_list[position], volt_grad.T, preferred_element_type=jnp.floa...  11.4 us
  transfers between devices with their start and end apart: 2, of which 2 were waited for; matrix products, arithmetic and copies ran while one was open for 0% of the time, Pallas kernels for 0%

commit v1 on v0

--- a/solution.py
+++ b/solution.py
@@ -36,7 +36,7 @@
         partial_sum = jnp.sum(factor_volts * factor_volts, axis=0)
         partial_list.append(partial_sum)
     variance = jnp.stack(partial_list, axis=0).reshape(members, hours, -1)
-    variance = lax.psum(variance, "factor")
+    variance = jnp.sum(lax.all_gather(variance, "factor"), axis=0)
     deviation = jnp.sqrt(variance + epsilon)
     margin = headroom - quantile * deviation
     violation = jnp.maximum(-margin, 0.0)

time: 325 us -> 272 us (0.84)
  waiting for transfers between devices: 162 us -> 84.2 us
  blocking collectives: 49.2 us -> 77.6 us
    psum x1 -> x0, waiting for transfers between devices: 71 us -> none  [shards(): variance = lax.psum(variance, 'factor')]
    all_gather x0 -> x1, blocking collectives: none -> 28.4 us  [shards(): variance = jnp.sum(lax.all_gather(variance, 'factor'), axis=0)]
    reduce_scatter x1, waiting for transfers between devices: 91.1 us -> 84.1 us  [shards(): lax.psum_scatter(whole_term, 'feeder', scatter_dimension=0, tiled=True)]
  transfers between devices with their start and end apart: 2 -> 1, of which waited for: 2 -> 1; matrix products, arithmetic and copies ran while one was open for 0% -> 0% of each run, Pallas kernels for 0% -> 0%
where the time goes in v1:
time: 272 us; the launch traced here: 271 us
  waiting for transfers between devices  84.2 us (31%)
  blocking collectives  77.6 us (29%)
  local copies, waits for them, and re-layouts  65.7 us (24%)
  matrix products  24.1 us (9%)
  between operations  14.4 us (5%)
  other arithmetic  5.47 us (2%)
    reduce_scatter x1, waiting for transfers between devices, shards(): lax.psum_scatter(whole_term, 'feeder', scatter_dimension=0, tiled=True)  84.1 us
    gather x8, local copies, waits for them, and re-layouts, shards(): sens_rows = jnp.take(sensitivity[member], ev_node[member, interval], axis=0)  61 us
    all_gather x1, blocking collectives, shards(): shard_rows = lax.all_gather(packed, 'feeder', axis=0, tiled=True)  49.2 us
    all_gather x1, blocking collectives, shards(): variance = jnp.sum(lax.all_gather(variance, 'factor'), axis=0)  28.4 us
    dot_general x8, matrix products, shards(): jnp.dot(weighted.T, sens_rows, preferred_element_type=jnp.float32)  13.7 us
    dot_general x8, matrix products, shards(): jnp.dot(rows_list[position], volt_grad.T, preferred_element_type=jnp.floa...  10 us
  transfers between devices with their start and end apart: 1, of which 1 were waited for; matrix products, arithmetic and copies ran while one was open for 0% of the time, Pallas kernels for 0%

profile of v1, /device:TPU:2, one launch (start us, length us, event | category | flops | bytes accessed | tf_op | source)
XLA Modules:
  0.0 271.4 jit_solution(8871865781920652759)
XLA Ops:
  10.4 49.2 %all_gather.6 = bf16[512,512]{1,0:T(8,128)(2,1)S(1)} all-gather(bf16[16,512]{1,0:T(8,128)(2,1)S(1)} %reshape.159), channel_id=1, replica_groups=mesh['feeder'=32,'factor'=8] {'feeder'}, dimensions={0}, use_global_device_ids=true | all-gather | bytes 540672 | tf_op jit(solution)/shard_map/all_gather | solution.py:18
  59.6 6.8 %gather_fusion.2 = bf16[256,2048]{1,0:T(8,128)(2,1)S(1)} fusion(bf16[2048,2048]{1,0:T(8,128)(2,1)} %bitcast.45, s32[1024]{0:T(1024)S(1)} %pad_clamp_fusion.5), kind=kCustom, calls=%fused_computation.2.clone | custom fusion | bytes 2098176 | tf_op jit(solution)/shard_map/jit(_take)/gather | solution.py:32
  66.4 6.8 %gather_fusion.3 = bf16[256,2048]{1,0:T(8,128)(2,1)S(1)} fusion(bf16[2048,2048]{1,0:T(8,128)(2,1)} %bitcast.46, s32[1024]{0:T(1024)S(1)} %pad_clamp_fusion.4), kind=kCustom, calls=%fused_computation.3.clone | custom fusion | bytes 2098176 | tf_op jit(solution)/shard_map/jit(_take)/gather | solution.py:32
  73.3 7.8 %gather_fusion.4 = bf16[256,2048]{1,0:T(8,128)(2,1)} fusion(bf16[2048,2048]{1,0:T(8,128)(2,1)} %bitcast.47, s32[1024]{0:T(1024)S(1)} %pad_clamp_fusion.3), kind=kCustom, calls=%fused_computation.4.clone | custom fusion | bytes 2098176 | tf_op jit(solution)/shard_map/jit(_take)/gather | solution.py:32
  81.1 8.0 %gather_fusion.5 = bf16[256,2048]{1,0:T(8,128)(2,1)} fusion(bf16[2048,2048]{1,0:T(8,128)(2,1)} %bitcast.48, s32[1024]{0:T(1024)S(1)} %pad_clamp_fusion.2), kind=kCustom, calls=%fused_computation.5.clone | custom fusion | bytes 2098176 | tf_op jit(solution)/shard_map/jit(_take)/gather | solution.py:32
  89.1 7.8 %gather_fusion.6 = bf16[256,2048]{1,0:T(8,128)(2,1)} fusion(bf16[2048,2048]{1,0:T(8,128)(2,1)} %bitcast.49, s32[1024]{0:T(1024)S(1)} %pad_clamp_fusion.1), kind=kCustom, calls=%fused_computation.6.clone | custom fusion | bytes 2098176 | tf_op jit(solution)/shard_map/jit(_take)/gather | solution.py:32
  96.9 7.8 %gather_fusion.7 = bf16[256,2048]{1,0:T(8,128)(2,1)} fusion(bf16[2048,2048]{1,0:T(8,128)(2,1)} %bitcast.50, s32[1024]{0:T(1024)S(1)} %pad_clamp_fusion), kind=kCustom, calls=%fused_computation.7.clone | custom fusion | bytes 2098176 | tf_op jit(solution)/shard_map/jit(_take)/gather | solution.py:32
  104.7 7.9 %gather_fusion.1 = bf16[256,2048]{1,0:T(8,128)(2,1)} fusion(bf16[2048,2048]{1,0:T(8,128)(2,1)} %bitcast.51, s32[1024]{0:T(1024)S(1)} %pad_clamp_fusion.6), kind=kCustom, calls=%fused_computation.1.clone | custom fusion | bytes 2098176 | tf_op jit(solution)/shard_map/jit(_take)/gather | solution.py:32
  112.6 8.0 %gather_fusion = bf16[256,2048]{1,0:T(8,128)(2,1)} fusion(bf16[2048,2048]{1,0:T(8,128)(2,1)} %bitcast.52, s32[1024]{0:T(1024)S(1)} %pad_clamp_fusion.7), kind=kCustom, calls=%fused_computation.clone | custom fusion | bytes 2098176 | tf_op jit(solution)/shard_map/jit(_take)/gather | solution.py:32
  121.0 1.2 multiply_reduce_fusion.5
  122.3 1.2 multiply_reduce_fusion.4
  123.5 2.5 multiply_reduce_fusion.3
  126.0 2.6 multiply_reduce_fusion.2
  128.6 2.4 multiply_reduce_fusion.1
  131.0 1.3 multiply_reduce_fusion
  132.3 1.3 multiply_reduce_fusion.6
  133.5 1.2 multiply_reduce_fusion.7
  134.9 28.4 %all-gather = f32[64,2048]{1,0:T(8,128)S(1)} all-gather(f32[8,2048]{1,0:T(8,128)S(1)} %stack.35), channel_id=2, replica_groups=mesh['feeder'=32,'factor'=8] {'factor'}, dimensions={0}, use_global_device_ids=true | all-gather | bytes 589824 | tf_op jit(solution)/shard_map/all_gather | solution.py:39
  164.1 2.0 convolution_multiply_fusion
  166.0 1.8 convolution_multiply_fusion.1
  167.9 2.5 convolution_multiply_fusion.2
  174.2 1.3 concatenate.3
  175.5 2.3 scatter_custom_fusion
  179.0 84.1 %reduce-scatter.2.cloned.1.call-done = f32[16,512]{1,0:T(8,128)} async-done(((f32[512,512]{1,0:T(8,128)}), f32[16,512]{1,0:T(8,128)}) %reduce-scatter.2.cloned.1.call-update) | async-done | bytes 32784 | tf_op jit(solution)/shard_map/reduce_scatter | solution.py:59
  (73 shorter events, 10.7 us)
Async XLA Ops:
  7.2 255.9 %reduce-scatter.2.cloned.1.call-start = ((), (), s32[]{:S(2)}) async-start(), calls=%async_computation.1 | async-start | bytes 1081344 | tf_op jit(solution)/shard_map/reduce_scatter | solution.py:59
  104.7 15.9 %copy-start.8 = (s32[1,256]{1,0:T(1,128)S(1)}, s32[1,256]{1,0:T(1,128)}, u32[]{:S(2)}) copy-start(s32[1,256]{1,0:T(1,128)} %param.12) | copy-start | bytes 3076
  120.6 10.4 %copy-start.5 = (bf16[256,2048]{1,0:T(8,128)(2,1)S(1)}, bf16[256,2048]{1,0:T(8,128)(2,1)}, u32[]{:S(2)}) copy-start(bf16[256,2048]{1,0:T(8,128)(2,1)} %gather_fusion.7) | copy-start | bytes 3145732
  120.6 11.6 %copy-start.2 = (bf16[256,2048]{1,0:T(8,128)(2,1)S(1)}, bf16[256,2048]{1,0:T(8,128)(2,1)}, u32[]{:S(2)}) copy-start(bf16[256,2048]{1,0:T(8,128)(2,1)} %gather_fusion.1) | copy-start | bytes 3145732
  120.6 12.9 %copy-start = (bf16[256,2048]{1,0:T(8,128)(2,1)S(1)}, bf16[256,2048]{1,0:T(8,128)(2,1)}, u32[]{:S(2)}) copy-start(bf16[256,2048]{1,0:T(8,128)(2,1)} %gather_fusion) | copy-start | bytes 3145732
  120.6 42.7 %copy-start.7 = (f32[1,8,2048]{2,1,0:T(8,128)S(1)}, f32[1,8,2048]{2,1,0:T(8,128)}, u32[]{:S(2)}) copy-start(f32[1,8,2048]{2,1,0:T(8,128)} %param.9) | copy-start | bytes 196612
  134.8 38.4 %copy-start.3 = (bf16[256,2048]{1,0:T(8,128)(2,1)S(1)}, bf16[256,2048]{1,0:T(8,128)(2,1)}, u32[]{:S(2)}) copy-start(bf16[256,2048]{1,0:T(8,128)(2,1)} %gather_fusion.1) | copy-start | bytes 3145732
  134.9 35.5 %copy-start.4 = (bf16[256,2048]{1,0:T(8,128)(2,1)S(1)}, bf16[256,2048]{1,0:T(8,128)(2,1)}, u32[]{:S(2)}) copy-start(bf16[256,2048]{1,0:T(8,128)(2,1)} %gather_fusion.4) | copy-start | bytes 3145732
  134.9 35.5 %copy-start.13 = (f32[64,2048]{1,0:T(8,128)S(1)}, f32[64,2048]{1,0:T(8,128)}, u32[]{:S(2)}) copy-start(f32[64,2048]{1,0:T(8,128)} %get-tuple-element.38) | copy-start | bytes 1572868
  134.9 36.6 %copy-start.11 = (f32[64,2048]{1,0:T(8,128)S(1)}, f32[64,2048]{1,0:T(8,128)}, u32[]{:S(2)}) copy-start(f32[64,2048]{1,0:T(8,128)} %get-tuple-element.36) | copy-start | bytes 1572868
  134.9 37.8 %copy-start.9 = (f32[64,2048]{1,0:T(8,128)S(1)}, f32[64,2048]{1,0:T(8,128)}, u32[]{:S(2)}) copy-start(f32[64,2048]{1,0:T(8,128)} %get-tuple-element.34) | copy-start | bytes 1572868
  134.9 38.3 %copy-start.12 = (f32[64,2048]{1,0:T(8,128)S(1)}, f32[64,2048]{1,0:T(8,128)}, u32[]{:S(2)}) copy-start(f32[64,2048]{1,0:T(8,128)} %get-tuple-element.32) | copy-start | bytes 1572868
  164.1 9.6 %copy-start.1 = (bf16[256,2048]{1,0:T(8,128)(2,1)S(1)}, bf16[256,2048]{1,0:T(8,128)(2,1)}, u32[]{:S(2)}) copy-start(bf16[256,2048]{1,0:T(8,128)(2,1)} %gather_fusion) | copy-start | bytes 3145732
  164.1 9.6 %copy-start.10 = (f32[64,2048]{1,0:T(8,128)S(1)}, f32[64,2048]{1,0:T(8,128)}, u32[]{:S(2)}) copy-start(f32[64,2048]{1,0:T(8,128)} %get-tuple-element.30) | copy-start | bytes 1572868
  170.4 93.6 %copy-start.6 = (f32[16,8,64]{2,1,0:T(8,128)S(1)}, f32[16,8,64]{2,1,0:T(8,128)}, u32[]{:S(2)}) copy-start(f32[16,8,64]{2,1,0:T(8,128)} %param.13) | copy-start | bytes 98308
Sparse Core Ops, SparseCore 0:
  179.1 83.9 reduce-scatter.1
